TPU v7x, 256 devices: a whole 4x4x8 slice. The times are simulated.
256 devices in a mesh: seq: 64 (over z, y, core), tensor: 4 (over x).
Axes of the slice: x: 4, y: 4, z: 8, core: 2. Of those that a mesh axis runs over, the one named last changes fastest.
Arguments:
- new_states: bfloat16 [4, 128, 1024], P(None, None, 'tensor'), may hold values from -6 to 6
- self_query: bfloat16 [1024, 1024], P(None, 'tensor'), may hold values from -0.1875 to 0.1875
- self_key: bfloat16 [1024, 1024], P(None, 'tensor'), may hold values from -0.375 to 0.375
- self_value: bfloat16 [1024, 1024], P(None, 'tensor'), may hold values from -0.1875 to 0.1875
- self_output: bfloat16 [1024, 1024], P('tensor'), may hold values from -0.1875 to 0.1875
- cross_query: bfloat16 [1024, 1024], P(None, 'tensor'), may hold values from -0.1875 to 0.1875
- cross_output: bfloat16 [1024, 1024], P('tensor'), may hold values from -0.1875 to 0.1875
- feed_up: bfloat16 [1024, 4096], P(None, 'tensor'), may hold values from -0.1875 to 0.1875
- feed_down: bfloat16 [4096, 1024], P('tensor'), may hold values from -0.09375 to 0.09375
- norm_self: float32 [1024], replicated, may hold values from 0.25 to 1.75
- norm_cross: float32 [1024], replicated, may hold values from 0.25 to 1.75
- norm_feed: float32 [1024], replicated, may hold values from 0.25 to 1.75
- self_cache: bfloat16 [1536, 2, 128, 1024], P('seq', None, None, 'tensor'), may hold values from -240 to 240
- cross_cache: bfloat16 [128, 2, 512, 1024], P(None, None, 'seq', 'tensor'), may hold values from -240 to 240
- cache_lengths: int32 [128], replicated, may hold values from 1 to 16384, as said below
- page_table: int32 [128, 128], replicated, may hold values from -1 to 1535, as said below
- request_order: int32 [128], replicated, may hold values from 0 to 127, each once
- encoder_lengths: int32 [128], replicated, may hold values from 1 to 512, as said below
Outputs:
- out: bfloat16 [4, 128, 1024], P(None, None, 'tensor')
Inputs may be any that keep to these rules, and one draw needn't show every extreme that they name: `cache_lengths`: one request has exactly 16384 cached tokens. `page_table`: row r holds the slots of request r's pages in order: its first ceil(cache_lengths[r] / 128) entries are slots, page p holding positions p * 128 to (p + 1) * 128 - 1, and no slot appears twice in the table; the other entries are -1. Slot s belongs to seq index s // 24. `encoder_lengths`: one request has exactly 512 encoder positions.
All inputs are finite; a program needn't handle non-finite values.
Results may differ from a plain program's by a relative error of at most 0.014.
The roundings to bfloat16 on the way count: a program that leaves them out, or rounds other values in their place, can miss the bound.
Values may be sent and summed in bfloat16 or wider, within the bound.
No kernel may reach another device: no remote copies, remote signals or barrier semaphores. Data moves between devices by JAX's collectives and lax.ppermute only.
A program may use at most 64 MiB of HBM per device.

v0:
```python
import jax
import jax.numpy as jnp
from jax import lax
from jax.sharding import PartitionSpec as P

HEAD_DIM = 64


EPSILON = 1e-05
NEG_FILL = -1e30


def layer_norm(summed, gain):
    center = jnp.mean(summed, axis=-1, keepdims=True)
    spread = jnp.mean(summed * summed, axis=-1, keepdims=True) - center * center
    return (summed - center) * lax.rsqrt(spread + EPSILON) * gain


def global_max(local_max):
    return lax.pmax(local_max, "seq")


def global_totals(denom, numer):
    return lax.psum((denom, numer), "seq")


def reduce_norm(residual, partial_value, gain):
    width = residual.shape[1]
    total = lax.psum(partial_value, "tensor")
    full = layer_norm(residual.astype(jnp.float32) + total, gain).astype(jnp.bfloat16)
    columns = width // lax.axis_size("tensor")
    return (full, lax.dynamic_slice_in_dim(full, lax.axis_index("tensor") * columns, columns, 1))


def on_device(
    new_states,
    self_query,
    self_key,
    self_value,
    self_output,
    cross_query,
    cross_output,
    feed_up,
    feed_down,
    norm_self,
    norm_cross,
    norm_feed,
    self_cache,
    cross_cache,
    cache_lengths,
    page_table,
    request_order,
    encoder_lengths,
):
    states = lax.all_gather(new_states, "tensor", axis=2, tiled=True)
    steps, requests, width = states.shape
    flat = states.reshape(steps * requests, width)
    local_width = self_query.shape[1]
    local_heads = local_width // HEAD_DIM
    scaling = HEAD_DIM ** (-0.5)
    queries = (jnp.dot(flat, self_query, preferred_element_type=jnp.float32) * scaling).astype(
        jnp.bfloat16
    )
    new_keys = jnp.dot(flat, self_key, preferred_element_type=jnp.float32).astype(jnp.bfloat16)
    new_values = jnp.dot(flat, self_value, preferred_element_type=jnp.float32).astype(jnp.bfloat16)
    query_grid = queries.reshape(steps, requests, local_heads, HEAD_DIM)
    key_grid = new_keys.reshape(steps, requests, local_heads, HEAD_DIM)
    value_grid = new_values.reshape(steps, requests, local_heads, HEAD_DIM)
    slot_count = self_cache.shape[0]
    page_width = self_cache.shape[2]
    max_pages = page_table.shape[1]
    seq_index = lax.axis_index("seq")
    flat_table = page_table.reshape(-1)
    entry_ids = jnp.arange(requests * max_pages, dtype=jnp.int32)
    entry_request = entry_ids // max_pages
    entry_page = entry_ids % max_pages
    slot_ids = seq_index * slot_count + jnp.arange(slot_count, dtype=jnp.int32)
    matches = flat_table[None, :] == slot_ids[:, None]
    slot_live = jnp.any(matches, axis=1)
    slot_owner = jnp.sum(jnp.where(matches, entry_request[None, :], 0), axis=1)
    slot_page = jnp.sum(jnp.where(matches, entry_page[None, :], 0), axis=1)
    request_ids = jnp.arange(requests, dtype=jnp.int32)
    slot_length = jnp.sum(
        jnp.where(slot_owner[:, None] == request_ids[None, :], cache_lengths[None, :], 0), axis=1
    )
    positions = slot_page[:, None] * page_width + jnp.arange(page_width, dtype=jnp.int32)[None, :]
    slot_valid = slot_live[:, None] & (positions < slot_length[:, None])
    slot_rows = slot_live[:, None] & (request_order[None, :] == slot_owner[:, None])
    rows_half = slot_rows.astype(jnp.bfloat16)
    rows_wide = slot_rows.astype(jnp.float32)
    slot_query = jnp.einsum(
        "pb,sbc->psc",
        rows_half,
        queries.reshape(steps, requests, local_width),
        preferred_element_type=jnp.float32,
    ).astype(jnp.bfloat16)
    slot_query = slot_query.reshape(slot_count, steps, local_heads, HEAD_DIM)
    cache_keys = self_cache[:, 0].reshape(slot_count, page_width, local_heads, HEAD_DIM)
    cache_values = self_cache[:, 1].reshape(slot_count, page_width, local_heads, HEAD_DIM)
    cache_scores = jnp.einsum(
        "pshd,pkhd->pshk", slot_query, cache_keys, preferred_element_type=jnp.float32
    )
    valid_grid = slot_valid[:, None, None, :]
    slot_max = jnp.max(jnp.where(valid_grid, cache_scores, NEG_FILL), axis=3)
    row_max = jnp.max(
        jnp.where(slot_rows[:, None, :, None], slot_max[:, :, None, :], NEG_FILL), axis=0
    )
    causal = jnp.arange(steps)[None, :] <= jnp.arange(steps)[:, None]
    new_scores = jnp.einsum(
        "tbhd,ubhd->bhtu", query_grid, key_grid, preferred_element_type=jnp.float32
    )
    new_scores = jnp.where(causal, new_scores, NEG_FILL)
    new_max = jnp.transpose(jnp.max(new_scores, axis=3), (2, 0, 1))
    top = global_max(jnp.maximum(row_max, new_max))
    slot_top = jnp.einsum("pb,sbh->psh", rows_wide, top, precision=lax.Precision.HIGHEST)
    cache_weights = jnp.exp(jnp.where(valid_grid, cache_scores - slot_top[..., None], NEG_FILL))
    cache_denom = jnp.sum(cache_weights, axis=3)
    cache_numer = jnp.einsum(
        "pshk,pkhd->pshd",
        cache_weights.astype(jnp.bfloat16),
        cache_values,
        preferred_element_type=jnp.float32,
    )
    row_denom = jnp.einsum("pb,psh->sbh", rows_wide, cache_denom, precision=lax.Precision.HIGHEST)
    row_numer = jnp.einsum("pb,pshd->sbhd", rows_wide, cache_numer, precision=lax.Precision.HIGHEST)
    total_denom, total_numer = global_totals(row_denom, row_numer)
    top_new = jnp.transpose(top, (1, 2, 0))[..., None]
    new_weights = jnp.where(causal, jnp.exp(new_scores - top_new), 0.0)
    new_denom = jnp.transpose(jnp.sum(new_weights, axis=3), (2, 0, 1))
    new_numer = jnp.einsum(
        "bhtu,ubhd->tbhd",
        new_weights.astype(jnp.bfloat16),
        value_grid,
        preferred_element_type=jnp.float32,
    )
    self_attn = ((total_numer + new_numer) / (total_denom + new_denom)[..., None]).astype(
        jnp.bfloat16
    )
    partial_value = jnp.dot(
        self_attn.reshape(steps * requests, local_width),
        self_output,
        preferred_element_type=jnp.float32,
    )
    first_full, first_share = reduce_norm(flat, partial_value, norm_self)
    cross_queries = (
        jnp.dot(first_full, cross_query, preferred_element_type=jnp.float32) * scaling
    ).astype(jnp.bfloat16)
    cross_grid = cross_queries.reshape(steps, requests, local_heads, HEAD_DIM)
    order_rows = (request_order[:, None] == request_ids[None, :]).astype(jnp.bfloat16)
    request_query = jnp.einsum(
        "br,sbhd->srhd", order_rows, cross_grid, preferred_element_type=jnp.float32
    ).astype(jnp.bfloat16)
    enc_local = cross_cache.shape[2]
    enc_keys = cross_cache[:, 0].reshape(requests, enc_local, local_heads, HEAD_DIM)
    enc_values = cross_cache[:, 1].reshape(requests, enc_local, local_heads, HEAD_DIM)
    enc_positions = seq_index * enc_local + jnp.arange(enc_local, dtype=jnp.int32)
    enc_valid = (enc_positions[None, :] < encoder_lengths[:, None])[None, :, None, :]
    enc_scores = jnp.einsum(
        "srhd,rehd->srhe", request_query, enc_keys, preferred_element_type=jnp.float32
    )
    enc_top = global_max(jnp.max(jnp.where(enc_valid, enc_scores, NEG_FILL), axis=3))
    enc_weights = jnp.exp(jnp.where(enc_valid, enc_scores - enc_top[..., None], NEG_FILL))
    enc_numer_local = jnp.einsum(
        "srhe,rehd->srhd",
        enc_weights.astype(jnp.bfloat16),
        enc_values,
        preferred_element_type=jnp.float32,
    )
    enc_denom, enc_numer = global_totals(jnp.sum(enc_weights, axis=3), enc_numer_local)
    enc_attn = (enc_numer / enc_denom[..., None]).astype(jnp.bfloat16)
    cross_attn = jnp.einsum(
        "br,srhd->sbhd", order_rows, enc_attn, preferred_element_type=jnp.float32
    ).astype(jnp.bfloat16)
    partial_value = jnp.dot(
        cross_attn.reshape(steps * requests, local_width),
        cross_output,
        preferred_element_type=jnp.float32,
    )
    second_full, second_share = reduce_norm(first_full, partial_value, norm_cross)
    ffn_hidden = jax.nn.gelu(
        jnp.dot(second_full, feed_up, preferred_element_type=jnp.float32), approximate=False
    ).astype(jnp.bfloat16)
    ignored, out_share = reduce_norm(
        second_full, jnp.dot(ffn_hidden, feed_down, preferred_element_type=jnp.float32), norm_feed
    )
    return out_share.reshape(steps, requests, out_share.shape[1])


def solution(mesh):
    in_specs = (
        P(None, None, "tensor"),
        P(None, "tensor"),
        P(None, "tensor"),
        P(None, "tensor"),
        P("tensor", None),
        P(None, "tensor"),
        P("tensor", None),
        P(None, "tensor"),
        P("tensor", None),
        P(),
        P(),
        P(),
        P("seq", None, None, "tensor"),
        P(None, None, "seq", "tensor"),
        P(),
        P(),
        P(),
        P(),
    )
    out_specs = P(None, None, "tensor")
    return jax.shard_map(
        on_device, mesh=mesh, in_specs=in_specs, out_specs=out_specs, check_vma=False
    )
```

profile of v0, /device:TPU:1, one launch (start us, length us, event | category | flops | bytes accessed | tf_op | source)
XLA Modules:
  0.0 1101.1 jit_solution(13234853274242562757)
XLA Ops:
  7.3 3.9 fusion.134
  11.2 2.6 copy.103
  13.8 2.7 copy.147
  17.8 21.5 %all-gather.2.cloned.1.call-done = bf16[4,128,1024]{2,1,0:T(8,128)(2,1)} async-done(((bf16[4,128,256]{2,1,0:T(8,128)(2,1)}), bf16[4,128,1024]{2,1,0:T(8,128)(2,1)}) %all-gather.2.cloned.1.call-update) | async-done | bytes 1048592 | tf_op jit(solution)/shard_map/all_gather | solution.py:55
  44.4 2.2 convolution_convert_fusion.3
  48.7 3.0 fusion.62
  53.6 128.2 %pmax.14 = f32[4,128,4]{1,2,0:T(4,128)S(1)} all-reduce(f32[4,128,4]{1,2,0:T(4,128)S(1)} %fusion.99), channel_id=1, replica_groups=mesh['seq'=64,'tensor'=4] {'seq'}, use_global_device_ids=true, to_apply=%region_7.8 | all-reduce | flops 2048 | bytes 16384 | tf_op jit(solution)/shard_map/pmax | solution.py:20
  182.7 2.4 convolution_bitcast_fusion.2
  193.8 129.3 %psum.50 = f32[4,128,4]{1,2,0:T(4,128)S(1)} all-reduce(f32[4,128,4]{1,2,0:T(4,128)S(1)} %convolution_bitcast_fusion.4), channel_id=1, replica_groups=mesh['seq'=64,'tensor'=4] {'seq'}, use_global_device_ids=true, to_apply=%region_10.11 | all-reduce | flops 2048 | bytes 16384 | tf_op jit(solution)/shard_map/psum | solution.py:24
  323.1 44.2 %all-reduce.6.cloned.1.call-done = f32[4,128,4,64]{1,3,2,0:T(8,128)} async-done(((f32[4,128,4,64]{1,3,2,0:T(8,128)}), f32[4,128,4,64]{1,3,2,0:T(8,128)}) %all-reduce.6.cloned.1.call-update) | async-done | bytes 524304 | tf_op jit(solution)/shard_map/psum | solution.py:24
  374.2 3.5 copy.129
  377.7 2.2 copy.149
  379.9 3.4 copy.131
  383.4 50.2 %all-reduce.8.cloned.1.call-done = f32[512,1024]{1,0:T(8,128)} async-done(((f32[512,1024]{1,0:T(8,128)}), f32[512,1024]{1,0:T(8,128)}) %all-reduce.8.cloned.1.call-update) | async-done | bytes 2097168 | tf_op jit(solution)/shard_map/psum | solution.py:29
  433.6 2.2 fusion.48
  441.2 4.0 select_reduce_fusion
  445.1 246.6 %pmax.15 = f32[4,128,4]{0,2,1:T(4,128)S(1)} all-reduce(f32[4,128,4]{0,2,1:T(4,128)} %get-tuple-element.30), channel_id=1, replica_groups=mesh['seq'=64,'tensor'=4] {'seq'}, use_global_device_ids=true, to_apply=%region_16.17 | all-reduce | flops 2048 | bytes 16384 | tf_op jit(solution)/shard_map/pmax | solution.py:20
  691.8 3.4 fusion.52
  695.2 2.4 copy.132
  697.7 3.1 fusion.50
  700.8 246.8 %psum.53 = f32[4,128,4]{0,2,1:T(4,128)S(1)} all-reduce(f32[4,128,4]{0,2,1:T(4,128)} %fusion.50), channel_id=1, replica_groups=mesh['seq'=64,'tensor'=4] {'seq'}, use_global_device_ids=true, to_apply=%region_19.20 | all-reduce | flops 2048 | bytes 16384 | tf_op jit(solution)/shard_map/psum | solution.py:24
  951.4 63.0 %all-reduce.12.cloned.1.call-done = f32[512,1024]{1,0:T(8,128)} async-done(((f32[512,1024]{1,0:T(8,128)}), f32[512,1024]{1,0:T(8,128)}) %all-reduce.12.cloned.1.call-update) | async-done | bytes 2097168 | tf_op jit(solution)/shard_map/psum | solution.py:29
  1018.1 9.5 fusion.16
  1028.5 62.9 %all-reduce.14.cloned.1.call-done = f32[512,1024]{1,0:T(8,128)} async-done(((f32[512,1024]{1,0:T(8,128)}), f32[512,1024]{1,0:T(8,128)}) %all-reduce.14.cloned.1.call-update) | async-done | bytes 2097168 | tf_op jit(solution)/shard_map/psum | solution.py:29
  (104 shorter events, 44.2 us)
Async XLA Ops:
  6.5 1011.5 %copy-start = (bf16[1024,1024]{1,0:T(8,128)(2,1)S(1)}, bf16[1024,1024]{1,0:T(8,128)(2,1)}, u32[]{:S(2)}) copy-start(bf16[1024,1024]{1,0:T(8,128)(2,1)} %param.26) | copy-start | bytes 6291460
  6.5 32.7 %all-gather.2.cloned.1.call-start = ((), (), s32[]{:S(2)}) async-start(), calls=%async_computation | async-start | bytes 1310720 | tf_op jit(solution)/shard_map/all_gather | solution.py:55
  7.3 360.1 %all-reduce.6.cloned.1.call-start = ((), (), s32[]{:S(2)}) async-start(), calls=%async_computation.1 | async-start | bytes 1048576 | tf_op jit(solution)/shard_map/psum | solution.py:24
  13.8 2.7 copy-start.9
  13.8 3.3 copy-start.16
  13.8 3.9 copy-start.10
  13.8 25.4 %copy-start.14 = (bf16[1024,256]{1,0:T(8,128)(2,1)S(1)}, bf16[1024,256]{1,0:T(8,128)(2,1)}, u32[]{:S(2)}) copy-start(bf16[1024,256]{1,0:T(8,128)(2,1)} %param.19) | copy-start | bytes 1572868
  40.9 3.5 copy-start.3
  186.6 247.0 %all-reduce.8.cloned.1.call-start = ((), (), s32[]{:S(2)}) async-start(), calls=%async_computation.2 | async-start | bytes 4194304 | tf_op jit(solution)/shard_map/psum | solution.py:29
  193.7 175.1 %copy-start.7 = (bf16[256,1024]{1,0:T(8,128)(2,1)S(1)}, bf16[256,1024]{1,0:T(8,128)(2,1)}, u32[]{:S(2)}) copy-start(bf16[256,1024]{1,0:T(8,128)(2,1)} %param.22) | copy-start | bytes 1572868
  370.7 577.0 %all-reduce.10.cloned.1.call-start = ((), (), s32[]{:S(2)}) async-start(), calls=%async_computation.3 | async-start | bytes 1048576 | tf_op jit(solution)/shard_map/psum | solution.py:24
  374.2 9.1 copy-start.13
  374.2 59.4 %copy-start.4 = (bf16[4,128,1024]{2,1,0:T(8,128)(2,1)S(1)}, bf16[4,128,1024]{2,1,0:T(8,128)(2,1)}, u32[]{:S(2)}) copy-start(bf16[4,128,1024]{2,1,0:T(8,128)(2,1)} %all-gather.2.cloned.1.call-done) | copy-start | bytes 3145732
  379.9 55.9 %copy-start.11 = (f32[1024]{0:T(1024)S(1)}, f32[1024]{0:T(1024)}, u32[]{:S(2)}) copy-start(f32[1024]{0:T(1024)} %param.27) | copy-start | bytes 12292
  433.6 2.2 copy-start.1
  433.6 2.5 copy-start.5
  436.1 1.0 copy-start.15
  697.6 316.8 %all-reduce.12.cloned.1.call-start = ((), (), s32[]{:S(2)}) async-start(), calls=%async_computation.4 | async-start | bytes 4194304 | tf_op jit(solution)/shard_map/psum | solution.py:29
  947.7 1.7 copy-start.8
  951.1 65.5 %copy-start.12 = (f32[1024]{0:T(1024)S(1)}, f32[1024]{0:T(1024)}, u32[]{:S(2)}) copy-start(f32[1024]{0:T(1024)} %param.28) | copy-start | bytes 12292
  951.1 140.2 %all-reduce.14.cloned.1.call-start = ((), (), s32[]{:S(2)}) async-start(), calls=%async_computation.5 | async-start | bytes 4194304 | tf_op jit(solution)/shard_map/psum | solution.py:29
  1014.4 2.2 copy-start.2
  1027.6 63.7 %copy-start.6 = (bf16[512,1024]{1,0:T(8,128)(2,1)S(1)}, bf16[512,1024]{1,0:T(8,128)(2,1)}, u32[]{:S(2)}) copy-start(bf16[512,1024]{1,0:T(8,128)(2,1)} %multiply_convert_fusion) | copy-start | bytes 3145732
Sparse Core Ops, SparseCore 0:
  9.1 30.0 all-gather.1
  186.7 180.5 all-reduce.5
  370.8 62.7 all-reduce.7
  697.7 181.0 all-reduce.9
  951.2 63.1 all-reduce.11
  1027.8 63.5 all-reduce.13
where the time goes:
time: 1100 us
  blocking collectives  751 us (68%)
  waiting for transfers between devices  243 us (22%)
  matrix products  40.3 us (4%)
  local copies, waits for them, and re-layouts  37.1 us (3%)
  other arithmetic  15.7 us (1%)
  between operations  13.8 us (1%)
    psum x2, blocking collectives, global_totals(): return lax.psum((denom, numer), 'seq')  376 us
    pmax x2, blocking collectives, global_max(): return lax.pmax(local_max, 'seq')  375 us
    psum x3, waiting for transfers between devices, reduce_norm(): total = lax.psum(partial_value, 'tensor')  176 us
    psum x2, waiting for transfers between devices, global_totals(): return lax.psum((denom, numer), 'seq')  44.2 us
  transfers between devices with their start and end apart: 6, of which 5 were waited for; matrix products, arithmetic and copies ran while one was open for 3% of the time, Pallas kernels for 0%

commit v1 on v0

--- a/solution.py
+++ b/solution.py
@@ -16,12 +16,21 @@
     return (summed - center) * lax.rsqrt(spread + EPSILON) * gain
 
 
-def global_max(local_max):
-    return lax.pmax(local_max, "seq")
+def global_max(local_max, size):
+    result = local_max
+    distance = 1
+    while distance < size:
+        pairs = [(i, i ^ distance) for i in range(size)]
+        result = jnp.maximum(result, lax.ppermute(result, "seq", pairs))
+        distance *= 2
+    return result
 
 
 def global_totals(denom, numer):
-    return lax.psum((denom, numer), "seq")
+    packed = jnp.concatenate([numer.reshape(-1), denom.reshape(-1)])
+    packed = lax.psum(packed, "seq")
+    count = numer.size
+    return (packed[count:].reshape(denom.shape), packed[:count].reshape(numer.shape))
 
 
 def reduce_norm(residual, partial_value, gain):
@@ -70,6 +79,7 @@
     page_width = self_cache.shape[2]
     max_pages = page_table.shape[1]
     seq_index = lax.axis_index("seq")
+    seq_size = lax.axis_size("seq")
     flat_table = page_table.reshape(-1)
     entry_ids = jnp.arange(requests * max_pages, dtype=jnp.int32)
     entry_request = entry_ids // max_pages
@@ -111,7 +121,7 @@
     )
     new_scores = jnp.where(causal, new_scores, NEG_FILL)
     new_max = jnp.transpose(jnp.max(new_scores, axis=3), (2, 0, 1))
-    top = global_max(jnp.maximum(row_max, new_max))
+    top = global_max(jnp.maximum(row_max, new_max), seq_size)
     slot_top = jnp.einsum("pb,sbh->psh", rows_wide, top, precision=lax.Precision.HIGHEST)
     cache_weights = jnp.exp(jnp.where(valid_grid, cache_scores - slot_top[..., None], NEG_FILL))
     cache_denom = jnp.sum(cache_weights, axis=3)
@@ -158,7 +168,7 @@
     enc_scores = jnp.einsum(
         "srhd,rehd->srhe", request_query, enc_keys, preferred_element_type=jnp.float32
     )
-    enc_top = global_max(jnp.max(jnp.where(enc_valid, enc_scores, NEG_FILL), axis=3))
+    enc_top = global_max(jnp.max(jnp.where(enc_valid, enc_scores, NEG_FILL), axis=3), seq_size)
     enc_weights = jnp.exp(jnp.where(enc_valid, enc_scores - enc_top[..., None], NEG_FILL))
     enc_numer_local = jnp.einsum(
         "srhe,rehd->srhd",

time: 1100 us -> 781 us (0.71)
  blocking collectives: 751 us -> 0 us
  waiting for transfers between devices: 243 us -> 605 us
  starting transfers between devices: 0.61 us -> 29.5 us
  local copies, waits for them, and re-layouts: 37.1 us -> 61.7 us
    psum x2 -> x0, blocking collectives: 376 us -> none  [global_totals(): return lax.psum((denom, numer), 'seq')]
    pmax x2 -> x0, blocking collectives: 375 us -> none  [global_max(): return lax.pmax(local_max, 'seq')]
    psum x2, waiting for transfers between devices: 44.2 us -> 362 us  [global_totals(): packed = lax.psum(packed, 'seq')]
    ppermute x0 -> x12, waiting for transfers between devices: none -> 36.4 us  [global_max(): result = jnp.maximum(result, lax.ppermute(result, 'seq', pairs))]
    ppermute x0 -> x12, starting transfers between devices: none -> 28.8 us  [global_max(): result = jnp.maximum(result, lax.ppermute(result, 'seq', pairs))]
    slice x1 -> x11, local copies, waits for them, and re-layouts: 2.07 us -> 13.7 us  [the longest x1 3.9 us: on_device(): self_cache[:, 1].reshape(slot_count, page_width, local_heads, HEAD_DIM)]
  transfers between devices with their start and end apart: 6 -> 18, of which waited for: 5 -> 16; matrix products, arithmetic and copies ran while one was open for 3% -> 4% of each run, Pallas kernels for 0% -> 0%
where the time goes in v1:
time: 781 us; the launch traced here: 771 us
  waiting for transfers between devices  605 us (77%)
  local copies, waits for them, and re-layouts  61.7 us (8%)
  matrix products  38.2 us (5%)
  starting transfers between devices  29.5 us (4%)
  other arithmetic  22.4 us (3%)
  between operations  14.3 us (2%)
    psum x2, waiting for transfers between devices, global_totals(): packed = lax.psum(packed, 'seq')  362 us
    psum x3, waiting for transfers between devices, reduce_norm(): total = lax.psum(partial_value, 'tensor')  182 us
    ppermute x12, waiting for transfers between devices, global_max(): result = jnp.maximum(result, lax.ppermute(result, 'seq', pairs))  36.4 us
    ppermute x12, starting transfers between devices, global_max(): result = jnp.maximum(result, lax.ppermute(result, 'seq', pairs))  28.8 us
    all_gather x1, waiting for transfers between devices, on_device(): states = lax.all_gather(new_states, 'tensor', axis=2, tiled=True)  24.1 us
  transfers between devices with their start and end apart: 18, of which 16 were waited for; matrix products, arithmetic and copies ran while one was open for 4% of the time, Pallas kernels for 0%

profile of v1, /device:TPU:1, one launch (start us, length us, event | category | flops | bytes accessed | tf_op | source)
XLA Modules:
  0.0 771.3 jit_solution(12482341161338022725)
XLA Ops:
  7.3 3.9 fusion.133
  11.2 2.6 copy.115
  15.2 24.1 %all-gather.2.cloned.1.call-done = bf16[4,128,1024]{2,1,0:T(8,128)(2,1)} async-done(((bf16[4,128,256]{2,1,0:T(8,128)(2,1)}), bf16[4,128,1024]{2,1,0:T(8,128)(2,1)}) %all-gather.2.cloned.1.call-update) | async-done | bytes 1048592 | tf_op jit(solution)/shard_map/all_gather | solution.py:64
  48.7 3.0 fusion.61
  59.2 2.7 collective-permute-start.2
  68.0 2.6 copy.164
  70.6 4.0 collective-permute-start.5
  93.5 179.7 %all-reduce.6.cloned.1.call-done = f32[133120]{0:T(1024)} async-done(((f32[133120]{0:T(1024)}), f32[133120]{0:T(1024)}) %all-reduce.6.cloned.1.call-update) | async-done | bytes 532496 | tf_op jit(solution)/shard_map/psum | solution.py:31
  291.5 3.4 copy.145
  294.9 55.6 %all-reduce.8.cloned.1.call-done = f32[512,1024]{1,0:T(8,128)} async-done(((f32[512,1024]{1,0:T(8,128)}), f32[512,1024]{1,0:T(8,128)}) %all-reduce.8.cloned.1.call-update) | async-done | bytes 2097168 | tf_op jit(solution)/shard_map/psum | solution.py:38
  358.2 3.2 select_reduce_fusion
  364.9 6.3 collective-permute-done.7
  371.3 2.8 collective-permute-start.8
  374.1 5.4 collective-permute-done.8
  380.9 4.5 collective-permute-done.9
  387.9 11.5 %collective-permute-done.10 = f32[4,128,4]{0,2,1:T(4,128)S(1)} collective-permute-done((f32[4,128,4]{0,2,1:T(4,128)S(1)}, f32[4,128,4]{0,2,1:T(4,128)S(1)}, u32[]{:S(2)}, u32[]{:S(2)}) %collective-permute-start.10) | collective-permute-done | bytes 8224 | tf_op jit(solution)/shard_map/ppermute | solution.py:24
  399.4 6.3 collective-permute-start.11
  407.9 3.4 copy.147
  411.3 2.9 collective-permute-done.11
  424.9 2.5 reshape.280
  429.4 182.2 %all-reduce.10.cloned.1.call-done = f32[133120]{0:T(1024)} async-done(((f32[133120]{0:T(1024)}), f32[133120]{0:T(1024)}) %all-reduce.10.cloned.1.call-update) | async-done | bytes 532496 | tf_op jit(solution)/shard_map/psum | solution.py:31
  620.7 63.4 %all-reduce.12.cloned.1.call-done = f32[512,1024]{1,0:T(8,128)} async-done(((f32[512,1024]{1,0:T(8,128)}), f32[512,1024]{1,0:T(8,128)}) %all-reduce.12.cloned.1.call-update) | async-done | bytes 2097168 | tf_op jit(solution)/shard_map/psum | solution.py:38
  687.8 9.5 %fusion.16 = f32[512,1024]{1,0:T(8,128)} fusion(bf16[1024,1024]{1,0:T(8,128)(2,1)S(1)} %copy-done, bf16[512,1024]{1,0:T(8,128)(2,1)} %multiply_convert_fusion, bf16[1024,1024]{1,0:T(8,128)(2,1)} %param.25), kind=kOutput, calls=%fused_computation.49 | convolution fusion | flops 2181562368 | bytes 7340032 | tf_op jit(solution)/shard_map/dot_general | solution.py:194
  698.2 62.9 %all-reduce.14.cloned.1.call-done = f32[512,1024]{1,0:T(8,128)} async-done(((f32[512,1024]{1,0:T(8,128)}), f32[512,1024]{1,0:T(8,128)}) %all-reduce.14.cloned.1.call-update) | async-done | bytes 2097168 | tf_op jit(solution)/shard_map/psum | solution.py:38
  (165 shorter events, 108.5 us)
Async XLA Ops:
  6.5 681.3 %copy-start = (bf16[1024,1024]{1,0:T(8,128)(2,1)S(1)}, bf16[1024,1024]{1,0:T(8,128)(2,1)}, u32[]{:S(2)}) copy-start(bf16[1024,1024]{1,0:T(8,128)(2,1)} %param.26) | copy-start | bytes 6291460
  6.5 32.7 %all-gather.2.cloned.1.call-start = ((), (), s32[]{:S(2)}) async-start(), calls=%async_computation | async-start | bytes 1310720 | tf_op jit(solution)/shard_map/all_gather | solution.py:64
  7.3 266.0 %all-reduce.6.cloned.1.call-start = ((), (), s32[]{:S(2)}) async-start(), calls=%async_computation.1 | async-start | bytes 1064960 | tf_op jit(solution)/shard_map/psum | solution.py:31
  11.2 28.1 %copy-start.17 = (bf16[1024,256]{1,0:T(8,128)(2,1)S(1)}, bf16[1024,256]{1,0:T(8,128)(2,1)}, u32[]{:S(2)}) copy-start(bf16[1024,256]{1,0:T(8,128)(2,1)} %param.19) | copy-start | bytes 1572868
  53.5 3.2 collective-permute-start
  56.7 2.5 collective-permute-start.1
  59.2 4.0 collective-permute-start.2
  63.2 2.5 collective-permute-start.3
  65.7 4.9 collective-permute-start.4
  70.6 8.2 %collective-permute-start.5 = (f32[4,128,4]{1,2,0:T(4,128)S(1)}, f32[4,128,4]{1,2,0:T(4,128)S(1)}, u32[]{:S(2)}, u32[]{:S(2)}) collective-permute-start(f32[4,128,4]{1,2,0:T(4,128)S(1)} %max.44), channel_id=1, source_target_pairs={{0,128},{4,132},{8,136},{12,140},{16,144},{20,148},{24,152},{28,15... | collective-permute-start | bytes 24584 | tf_op jit(solution)/shard_map/ppermute | solution.py:24
  88.6 261.9 %all-reduce.8.cloned.1.call-start = ((), (), s32[]{:S(2)}) async-start(), calls=%async_computation.2 | async-start | bytes 4194304 | tf_op jit(solution)/shard_map/psum | solution.py:38
  286.8 324.8 %all-reduce.10.cloned.1.call-start = ((), (), s32[]{:S(2)}) async-start(), calls=%async_computation.3 | async-start | bytes 1064960 | tf_op jit(solution)/shard_map/psum | solution.py:31
  286.9 63.7 %copy-start.4 = (bf16[4,128,1024]{2,1,0:T(8,128)(2,1)S(1)}, bf16[4,128,1024]{2,1,0:T(8,128)(2,1)}, u32[]{:S(2)}) copy-start(bf16[4,128,1024]{2,1,0:T(8,128)(2,1)} %all-gather.2.cloned.1.call-done) | copy-start | bytes 3145732
  291.5 61.3 %copy-start.14 = (f32[1024]{0:T(1024)S(1)}, f32[1024]{0:T(1024)}, u32[]{:S(2)}) copy-start(f32[1024]{0:T(1024)} %param.27) | copy-start | bytes 12292
  361.5 2.1 collective-permute-start.6
  363.6 7.6 collective-permute-start.7
  371.3 8.2 %collective-permute-start.8 = (f32[4,128,4]{0,2,1:T(4,128)S(1)}, f32[4,128,4]{0,2,1:T(4,128)S(1)}, u32[]{:S(2)}, u32[]{:S(2)}) collective-permute-start(f32[4,128,4]{0,2,1:T(4,128)S(1)} %max.47), channel_id=1, source_target_pairs={{0,16},{4,20},{8,24},{12,28},{16,0},{20,4},{24,8},{28,12},{32,48},... | collective-permute-start | bytes 24584 | tf_op jit(solution)/shard_map/ppermute | solution.py:24
  379.6 5.9 collective-permute-start.9
  385.5 13.8 %collective-permute-start.10 = (f32[4,128,4]{0,2,1:T(4,128)S(1)}, f32[4,128,4]{0,2,1:T(4,128)S(1)}, u32[]{:S(2)}, u32[]{:S(2)}) collective-permute-start(f32[4,128,4]{0,2,1:T(4,128)S(1)} %max.49), channel_id=1, source_target_pairs={{0,64},{4,68},{8,72},{12,76},{16,80},{20,84},{24,88},{28,92},{32,9... | collective-permute-start | bytes 24584 | tf_op jit(solution)/shard_map/ppermute | solution.py:24
  399.4 14.8 %collective-permute-start.11 = (f32[4,128,4]{0,2,1:T(4,128)S(1)}, f32[4,128,4]{0,2,1:T(4,128)}, u32[]{:S(2)}, u32[]{:S(2)}) collective-permute-start(f32[4,128,4]{0,2,1:T(4,128)S(1)} %max.50), channel_id=1, source_target_pairs={{0,128},{4,132},{8,136},{12,140},{16,144},{20,148},{24,152},{28,15... | collective-permute-start | bytes 24584 | tf_op jit(solution)/shard_map/ppermute | solution.py:24
  429.3 254.8 %all-reduce.12.cloned.1.call-start = ((), (), s32[]{:S(2)}) async-start(), calls=%async_computation.4 | async-start | bytes 4194304 | tf_op jit(solution)/shard_map/psum | solution.py:38
  620.4 65.9 %copy-start.15 = (f32[1024]{0:T(1024)S(1)}, f32[1024]{0:T(1024)}, u32[]{:S(2)}) copy-start(f32[1024]{0:T(1024)} %param.28) | copy-start | bytes 12292
  620.4 140.6 %all-reduce.14.cloned.1.call-start = ((), (), s32[]{:S(2)}) async-start(), calls=%async_computation.5 | async-start | bytes 4194304 | tf_op jit(solution)/shard_map/psum | solution.py:38
  697.3 63.7 %copy-start.6 = (bf16[512,1024]{1,0:T(8,128)(2,1)S(1)}, bf16[512,1024]{1,0:T(8,128)(2,1)}, u32[]{:S(2)}) copy-start(bf16[512,1024]{1,0:T(8,128)(2,1)} %multiply_convert_fusion) | copy-start | bytes 3145732
  (16 other events, 54.8 us)
Sparse Core Ops, SparseCore 0:
  9.1 30.0 all-gather.1
  88.8 184.4 all-reduce.5
  286.9 63.5 all-reduce.7
  429.5 182.0 all-reduce.9
  620.5 63.5 all-reduce.11
  697.4 63.5 all-reduce.13

commit v2 on v1

--- a/solution.py
+++ b/solution.py
@@ -16,21 +16,27 @@
     return (summed - center) * lax.rsqrt(spread + EPSILON) * gain
 
 
-def global_max(local_max, size):
-    result = local_max
+def combine_seq(top, denom, numer, size):
+    index = lax.axis_index("seq")
     distance = 1
     while distance < size:
         pairs = [(i, i ^ distance) for i in range(size)]
-        result = jnp.maximum(result, lax.ppermute(result, "seq", pairs))
+        other_top, other_denom, other_numer = lax.ppermute((top, denom, numer), "seq", pairs)
+        low = (index & distance) == 0
+        top_a = jnp.where(low, top, other_top)
+        top_b = jnp.where(low, other_top, top)
+        denom_a = jnp.where(low, denom, other_denom)
+        denom_b = jnp.where(low, other_denom, denom)
+        numer_a = jnp.where(low, numer, other_numer)
+        numer_b = jnp.where(low, other_numer, numer)
+        merged = jnp.maximum(top_a, top_b)
+        scale_a = jnp.exp(top_a - merged)
+        scale_b = jnp.exp(top_b - merged)
+        denom = denom_a * scale_a + denom_b * scale_b
+        numer = numer_a * scale_a[..., None] + numer_b * scale_b[..., None]
+        top = merged
         distance *= 2
-    return result
-
-
-def global_totals(denom, numer):
-    packed = jnp.concatenate([numer.reshape(-1), denom.reshape(-1)])
-    packed = lax.psum(packed, "seq")
-    count = numer.size
-    return (packed[count:].reshape(denom.shape), packed[:count].reshape(numer.shape))
+    return top, denom, numer
 
 
 def reduce_norm(residual, partial_value, gain):
@@ -121,8 +127,8 @@
     )
     new_scores = jnp.where(causal, new_scores, NEG_FILL)
     new_max = jnp.transpose(jnp.max(new_scores, axis=3), (2, 0, 1))
-    top = global_max(jnp.maximum(row_max, new_max), seq_size)
-    slot_top = jnp.einsum("pb,sbh->psh", rows_wide, top, precision=lax.Precision.HIGHEST)
+    local_top = jnp.maximum(row_max, new_max)
+    slot_top = jnp.einsum("pb,sbh->psh", rows_wide, local_top, precision=lax.Precision.HIGHEST)
     cache_weights = jnp.exp(jnp.where(valid_grid, cache_scores - slot_top[..., None], NEG_FILL))
     cache_denom = jnp.sum(cache_weights, axis=3)
     cache_numer = jnp.einsum(
@@ -133,7 +139,7 @@
     )
     row_denom = jnp.einsum("pb,psh->sbh", rows_wide, cache_denom, precision=lax.Precision.HIGHEST)
     row_numer = jnp.einsum("pb,pshd->sbhd", rows_wide, cache_numer, precision=lax.Precision.HIGHEST)
-    total_denom, total_numer = global_totals(row_denom, row_numer)
+    top, total_denom, total_numer = combine_seq(local_top, row_denom, row_numer, seq_size)
     top_new = jnp.transpose(top, (1, 2, 0))[..., None]
     new_weights = jnp.where(causal, jnp.exp(new_scores - top_new), 0.0)
     new_denom = jnp.transpose(jnp.sum(new_weights, axis=3), (2, 0, 1))
@@ -168,15 +174,17 @@
     enc_scores = jnp.einsum(
         "srhd,rehd->srhe", request_query, enc_keys, preferred_element_type=jnp.float32
     )
-    enc_top = global_max(jnp.max(jnp.where(enc_valid, enc_scores, NEG_FILL), axis=3), seq_size)
-    enc_weights = jnp.exp(jnp.where(enc_valid, enc_scores - enc_top[..., None], NEG_FILL))
+    enc_local_top = jnp.max(jnp.where(enc_valid, enc_scores, NEG_FILL), axis=3)
+    enc_weights = jnp.exp(jnp.where(enc_valid, enc_scores - enc_local_top[..., None], NEG_FILL))
     enc_numer_local = jnp.einsum(
         "srhe,rehd->srhd",
         enc_weights.astype(jnp.bfloat16),
         enc_values,
         preferred_element_type=jnp.float32,
     )
-    enc_denom, enc_numer = global_totals(jnp.sum(enc_weights, axis=3), enc_numer_local)
+    enc_top, enc_denom, enc_numer = combine_seq(
+        enc_local_top, jnp.sum(enc_weights, axis=3), enc_numer_local, seq_size
+    )
     enc_attn = (enc_numer / enc_denom[..., None]).astype(jnp.bfloat16)
     cross_attn = jnp.einsum(
         "br,srhd->sbhd", order_rows, enc_attn, preferred_element_type=jnp.float32

time: 781 us -> 519 us (0.66)
  waiting for transfers between devices: 605 us -> 328 us
  starting transfers between devices: 29.5 us -> 60.7 us
  local copies, waits for them, and re-layouts: 61.7 us -> 39.2 us
    psum x2 -> x0, waiting for transfers between devices: 362 us -> none  [global_totals(): packed = lax.psum(packed, 'seq')]
    ppermute x12 -> x36, waiting for transfers between devices: 36.4 us -> 132 us  [combine_seq(): lax.ppermute((top, denom, numer), 'seq', pairs)]
    ppermute x12 -> x36, starting transfers between devices: 28.8 us -> 60 us  [combine_seq(): lax.ppermute((top, denom, numer), 'seq', pairs)]
    add x0 -> x21, other arithmetic: none -> 12.6 us  [the longest x10 12.5 us: combine_seq(): numer = numer_a * scale_a[..., None] + numer_b * scale_b[..., None]]
    reshape x7 -> x0, local copies, waits for them, and re-layouts: 10.2 us -> none  [the longest x3 5.12 us: global_totals(): packed[:count].reshape(numer.shape)]
    psum x3, waiting for transfers between devices: 182 us -> 174 us  [reduce_norm(): total = lax.psum(partial_value, 'tensor')]
  transfers between devices with their start and end apart: 18 -> 40, of which waited for: 16 -> 27; matrix products, arithmetic and copies ran while one was open for 4% -> 8% of each run, Pallas kernels for 0% -> 0%
where the time goes in v2:
time: 519 us; the launch traced here: 509 us
  waiting for transfers between devices  328 us (63%)
  starting transfers between devices  60.7 us (12%)
  local copies, waits for them, and re-layouts  39.2 us (8%)
  matrix products  39.2 us (8%)
  other arithmetic  28.6 us (6%)
  between operations  13.8 us (3%)
    psum x3, waiting for transfers between devices, reduce_norm(): total = lax.psum(partial_value, 'tensor')  174 us
    ppermute x36, waiting for transfers between devices, combine_seq(): lax.ppermute((top, denom, numer), 'seq', pairs)  132 us
    ppermute x36, starting transfers between devices, combine_seq(): lax.ppermute((top, denom, numer), 'seq', pairs)  60 us
    all_gather x1, waiting for transfers between devices, on_device(): states = lax.all_gather(new_states, 'tensor', axis=2, tiled=True)  21.5 us
    add x10, other arithmetic, combine_seq(): numer = numer_a * scale_a[..., None] + numer_b * scale_b[..., None]  12.5 us
  transfers between devices with their start and end apart: 40, of which 27 were waited for; matrix products, arithmetic and copies ran while one was open for 8% of the time, Pallas kernels for 0%

profile of v2, /device:TPU:1, one launch (start us, length us, event | category | flops | bytes accessed | tf_op | source)
XLA Modules:
  0.0 509.1 jit_solution(6151670205311232972)
XLA Ops:
  7.3 3.9 fusion.159
  17.8 21.5 %all-gather.2.cloned.1.call-done = bf16[4,128,1024]{2,1,0:T(8,128)(2,1)} async-done(((bf16[4,128,256]{2,1,0:T(8,128)(2,1)}), bf16[4,128,1024]{2,1,0:T(8,128)(2,1)}) %all-gather.2.cloned.1.call-update) | async-done | bytes 1048592 | tf_op jit(solution)/shard_map/all_gather | solution.py:70
  66.9 11.0 %collective-permute-done.13 = f32[4,128,4]{1,2,0:T(4,128)S(1)} collective-permute-done((f32[4,128,4]{1,2,0:T(4,128)S(1)}, f32[4,128,4]{1,2,0:T(4,128)S(1)}, u32[]{:S(2)}, u32[]{:S(2)}) %collective-permute-start.13) | collective-permute-done | bytes 8224 | tf_op jit(solution)/shard_map/ppermute | solution.py:24
  85.9 8.7 %collective-permute-done.14 = f32[4,128,4]{1,2,0:T(4,128)S(1)} collective-permute-done((f32[4,128,4]{1,2,0:T(4,128)S(1)}, f32[4,128,4]{1,2,0:T(4,128)S(1)}, u32[]{:S(2)}, u32[]{:S(2)}) %collective-permute-start.14) | collective-permute-done | bytes 8224 | tf_op jit(solution)/shard_map/ppermute | solution.py:24
  99.9 9.4 %collective-permute-done.15 = f32[4,128,4]{1,2,0:T(4,128)S(1)} collective-permute-done((f32[4,128,4]{1,2,0:T(4,128)S(1)}, f32[4,128,4]{1,2,0:T(4,128)S(1)}, u32[]{:S(2)}, u32[]{:S(2)}) %collective-permute-start.15) | collective-permute-done | bytes 8224 | tf_op jit(solution)/shard_map/ppermute | solution.py:24
  116.3 3.8 collective-permute-start.11
  126.0 3.4 collective-permute-done.11
  129.4 10.9 %collective-permute-done.8 = f32[4,128,4,64]{1,3,2,0:T(8,128)} collective-permute-done((f32[4,128,4,64]{1,3,2,0:T(8,128)}, f32[4,128,4,64]{1,3,2,0:T(8,128)}, u32[]{:S(2)}, u32[]{:S(2)}) %collective-permute-start.8) | collective-permute-done | bytes 524320 | tf_op jit(solution)/shard_map/ppermute | solution.py:24
  142.5 6.2 %collective-permute-start.10 = (f32[4,128,4,64]{1,3,2,0:T(8,128)}, f32[4,128,4,64]{1,3,2,0:T(8,128)}, u32[]{:S(2)}, u32[]{:S(2)}) collective-permute-start(f32[4,128,4,64]{1,3,2,0:T(8,128)} %multiply_add_fusion.5), channel_id=1, source_target_pairs={{0,128},{4,132},{8,136},{12,140},{16,144},{20,148},{24,152},{28,15... | collective-permute-start | bytes 1572872 | tf_op jit(solution)/shard_map/ppermute | solution.py:24
  153.1 18.6 %collective-permute-done.10 = f32[4,128,4,64]{1,3,2,0:T(8,128)} collective-permute-done((f32[4,128,4,64]{1,3,2,0:T(8,128)}, f32[4,128,4,64]{1,3,2,0:T(8,128)}, u32[]{:S(2)}, u32[]{:S(2)}) %collective-permute-start.10) | collective-permute-done | bytes 524320 | tf_op jit(solution)/shard_map/ppermute | solution.py:24
  179.0 3.4 copy.146
  184.7 3.5 copy.148
  188.3 49.7 %all-reduce.4.cloned.1.call-done = f32[512,1024]{1,0:T(8,128)} async-done(((f32[512,1024]{1,0:T(8,128)}), f32[512,1024]{1,0:T(8,128)}) %all-reduce.4.cloned.1.call-update) | async-done | bytes 2097168 | tf_op jit(solution)/shard_map/psum | solution.py:44
  248.9 3.4 fusion.52
  265.2 10.6 %collective-permute-done.31 = f32[4,128,4]{1,2,0:T(4,128)S(1)} collective-permute-done((f32[4,128,4]{1,2,0:T(4,128)S(1)}, f32[4,128,4]{1,2,0:T(4,128)S(1)}, u32[]{:S(2)}, u32[]{:S(2)}) %collective-permute-start.31) | collective-permute-done | bytes 8224 | tf_op jit(solution)/shard_map/ppermute | solution.py:24
  282.2 8.3 %collective-permute-done.32 = f32[4,128,4]{1,2,0:T(4,128)S(1)} collective-permute-done((f32[4,128,4]{1,2,0:T(4,128)S(1)}, f32[4,128,4]{1,2,0:T(4,128)S(1)}, u32[]{:S(2)}, u32[]{:S(2)}) %collective-permute-start.32) | collective-permute-done | bytes 8224 | tf_op jit(solution)/shard_map/ppermute | solution.py:24
  293.6 8.9 %collective-permute-done.33 = f32[4,128,4]{1,2,0:T(4,128)S(1)} collective-permute-done((f32[4,128,4]{1,2,0:T(4,128)S(1)}, f32[4,128,4]{1,2,0:T(4,128)S(1)}, u32[]{:S(2)}, u32[]{:S(2)}) %collective-permute-start.33) | collective-permute-done | bytes 8224 | tf_op jit(solution)/shard_map/ppermute | solution.py:24
  307.5 20.9 %collective-permute-done.34 = f32[4,128,4]{1,2,0:T(4,128)S(1)} collective-permute-done((f32[4,128,4]{1,2,0:T(4,128)S(1)}, f32[4,128,4]{1,2,0:T(4,128)S(1)}, u32[]{:S(2)}, u32[]{:S(2)}) %collective-permute-start.34) | collective-permute-done | bytes 8224 | tf_op jit(solution)/shard_map/ppermute | solution.py:24
  328.7 6.4 %collective-permute-start.28 = (f32[4,128,4,64]{1,3,2,0:T(8,128)S(1)}, f32[4,128,4,64]{1,3,2,0:T(8,128)S(1)}, u32[]{:S(2)}, u32[]{:S(2)}) collective-permute-start(f32[4,128,4,64]{1,3,2,0:T(8,128)S(1)} %multiply_add_fusion), channel_id=1, source_target_pairs={{0,128},{4,132},{8,136},{12,140},{16,144},{20,148},{24,152},{28,15... | collective-permute-start | bytes 1572872 | tf_op jit(solution)/shard_map/ppermute | solution.py:24
  335.3 5.3 %collective-permute-start.29 = (f32[4,128,4]{1,2,0:T(4,128)S(1)}, f32[4,128,4]{1,2,0:T(4,128)S(1)}, u32[]{:S(2)}, u32[]{:S(2)}) collective-permute-start(f32[4,128,4]{1,2,0:T(4,128)S(1)} %bitcast.224), channel_id=1, source_target_pairs={{0,128},{4,132},{8,136},{12,140},{16,144},{20,148},{24,152},{28,15... | collective-permute-start | bytes 24584 | tf_op jit(solution)/shard_map/ppermute | solution.py:24
  340.5 18.0 %collective-permute-done.35 = f32[4,128,4]{1,2,0:T(4,128)S(1)} collective-permute-done((f32[4,128,4]{1,2,0:T(4,128)S(1)}, f32[4,128,4]{1,2,0:T(4,128)S(1)}, u32[]{:S(2)}, u32[]{:S(2)}) %collective-permute-start.35) | collective-permute-done | bytes 8224 | tf_op jit(solution)/shard_map/ppermute | solution.py:24
  361.4 61.2 %all-reduce.6.cloned.1.call-done = f32[512,1024]{1,0:T(8,128)} async-done(((f32[512,1024]{1,0:T(8,128)}), f32[512,1024]{1,0:T(8,128)}) %all-reduce.6.cloned.1.call-update) | async-done | bytes 2097168 | tf_op jit(solution)/shard_map/psum | solution.py:44
  426.2 9.5 %fusion.16 = f32[512,1024]{1,0:T(8,128)} fusion(bf16[1024,1024]{1,0:T(8,128)(2,1)S(1)} %copy-done, bf16[512,1024]{1,0:T(8,128)(2,1)} %multiply_convert_fusion, bf16[1024,1024]{1,0:T(8,128)(2,1)} %param.25), kind=kOutput, calls=%fused_computation.48 | convolution fusion | flops 2181562368 | bytes 7340032 | tf_op jit(solution)/shard_map/dot_general | solution.py:202
  436.6 62.9 %all-reduce.8.cloned.1.call-done = f32[512,1024]{1,0:T(8,128)} async-done(((f32[512,1024]{1,0:T(8,128)}), f32[512,1024]{1,0:T(8,128)}) %all-reduce.8.cloned.1.call-update) | async-done | bytes 2097168 | tf_op jit(solution)/shard_map/psum | solution.py:44
  (189 shorter events, 126.2 us)
Async XLA Ops:
  6.5 32.7 %all-gather.2.cloned.1.call-start = ((), (), s32[]{:S(2)}) async-start(), calls=%async_computation | async-start | bytes 1310720 | tf_op jit(solution)/shard_map/all_gather | solution.py:70
  7.3 230.7 %all-reduce.4.cloned.1.call-start = ((), (), s32[]{:S(2)}) async-start(), calls=%async_computation.1 | async-start | bytes 4194304 | tf_op jit(solution)/shard_map/psum | solution.py:44
  64.3 13.8 %collective-permute-start.2 = (f32[4,128,4,64]{1,3,2,0:T(8,128)}, f32[4,128,4,64]{1,3,2,0:T(8,128)}, u32[]{:S(2)}, u32[]{:S(2)}) collective-permute-start(f32[4,128,4,64]{1,3,2,0:T(8,128)} %multiply_add_fusion.9), channel_id=1, source_target_pairs={{0,8},{4,12},{8,0},{12,4},{16,24},{20,28},{24,16},{28,20},{32,40},... | collective-permute-start | bytes 1572872 | tf_op jit(solution)/shard_map/ppermute | solution.py:24
  65.5 12.4 %collective-permute-start.13 = (f32[4,128,4]{1,2,0:T(4,128)S(1)}, f32[4,128,4]{1,2,0:T(4,128)S(1)}, u32[]{:S(2)}, u32[]{:S(2)}) collective-permute-start(f32[4,128,4]{1,2,0:T(4,128)S(1)} %bitcast.233), channel_id=1, source_target_pairs={{0,8},{4,12},{8,0},{12,4},{16,24},{20,28},{24,16},{28,20},{32,40},... | collective-permute-start | bytes 24584 | tf_op jit(solution)/shard_map/ppermute | solution.py:24
  65.7 12.3 %collective-permute-start.3 = (f32[4,128,4]{1,2,0:T(4,128)S(1)}, f32[4,128,4]{1,2,0:T(4,128)S(1)}, u32[]{:S(2)}, u32[]{:S(2)}) collective-permute-start(f32[4,128,4]{1,2,0:T(4,128)S(1)} %bitcast.234), channel_id=1, source_target_pairs={{0,8},{4,12},{8,0},{12,4},{16,24},{20,28},{24,16},{28,20},{32,40},... | collective-permute-start | bytes 24584 | tf_op jit(solution)/shard_map/ppermute | solution.py:24
  80.2 14.6 %collective-permute-start.4 = (f32[4,128,4,64]{1,3,2,0:T(8,128)}, f32[4,128,4,64]{1,3,2,0:T(8,128)}, u32[]{:S(2)}, u32[]{:S(2)}) collective-permute-start(f32[4,128,4,64]{1,3,2,0:T(8,128)} %multiply_add_fusion.8), channel_id=1, source_target_pairs={{0,16},{4,20},{8,24},{12,28},{16,0},{20,4},{24,8},{28,12},{32,48},... | collective-permute-start | bytes 1572872 | tf_op jit(solution)/shard_map/ppermute | solution.py:24
  96.9 15.0 %collective-permute-start.6 = (f32[4,128,4,64]{1,3,2,0:T(8,128)}, f32[4,128,4,64]{1,3,2,0:T(8,128)}, u32[]{:S(2)}, u32[]{:S(2)}) collective-permute-start(f32[4,128,4,64]{1,3,2,0:T(8,128)} %multiply_add_fusion.7), channel_id=1, source_target_pairs={{0,32},{4,36},{8,40},{12,44},{16,48},{20,52},{24,56},{28,60},{32,0... | collective-permute-start | bytes 1572872 | tf_op jit(solution)/shard_map/ppermute | solution.py:24
  114.0 26.3 %collective-permute-start.8 = (f32[4,128,4,64]{1,3,2,0:T(8,128)}, f32[4,128,4,64]{1,3,2,0:T(8,128)}, u32[]{:S(2)}, u32[]{:S(2)}) collective-permute-start(f32[4,128,4,64]{1,3,2,0:T(8,128)} %multiply_add_fusion.6), channel_id=1, source_target_pairs={{0,64},{4,68},{8,72},{12,76},{16,80},{20,84},{24,88},{28,92},{32,9... | collective-permute-start | bytes 1572872 | tf_op jit(solution)/shard_map/ppermute | solution.py:24
  116.3 13.1 %collective-permute-start.11 = (f32[4,128,4]{1,2,0:T(4,128)S(1)}, f32[4,128,4]{1,2,0:T(4,128)S(1)}, u32[]{:S(2)}, u32[]{:S(2)}) collective-permute-start(f32[4,128,4]{1,2,0:T(4,128)S(1)} %bitcast.227), channel_id=1, source_target_pairs={{0,128},{4,132},{8,136},{12,140},{16,144},{20,148},{24,152},{28,15... | collective-permute-start | bytes 24584 | tf_op jit(solution)/shard_map/ppermute | solution.py:24
  124.4 28.7 %collective-permute-start.17 = (f32[4,128,4]{1,2,0:T(4,128)S(1)}, f32[4,128,4]{1,2,0:T(4,128)S(1)}, u32[]{:S(2)}, u32[]{:S(2)}) collective-permute-start(f32[4,128,4]{1,2,0:T(4,128)S(1)} %bitcast.229), channel_id=1, source_target_pairs={{0,128},{4,132},{8,136},{12,140},{16,144},{20,148},{24,152},{28,15... | collective-permute-start | bytes 24584 | tf_op jit(solution)/shard_map/ppermute | solution.py:24
  142.5 29.2 %collective-permute-start.10 = (f32[4,128,4,64]{1,3,2,0:T(8,128)}, f32[4,128,4,64]{1,3,2,0:T(8,128)}, u32[]{:S(2)}, u32[]{:S(2)}) collective-permute-start(f32[4,128,4,64]{1,3,2,0:T(8,128)} %multiply_add_fusion.5), channel_id=1, source_target_pairs={{0,128},{4,132},{8,136},{12,140},{16,144},{20,148},{24,152},{28,15... | collective-permute-start | bytes 1572872 | tf_op jit(solution)/shard_map/ppermute | solution.py:24
  175.3 247.2 %all-reduce.6.cloned.1.call-start = ((), (), s32[]{:S(2)}) async-start(), calls=%async_computation.2 | async-start | bytes 4194304 | tf_op jit(solution)/shard_map/psum | solution.py:44
  262.5 13.6 %collective-permute-start.20 = (f32[4,128,4,64]{1,3,2,0:T(8,128)S(1)}, f32[4,128,4,64]{1,3,2,0:T(8,128)S(1)}, u32[]{:S(2)}, u32[]{:S(2)}) collective-permute-start(f32[4,128,4,64]{1,3,2,0:T(8,128)S(1)} %multiply_add_fusion.4), channel_id=1, source_target_pairs={{0,8},{4,12},{8,0},{12,4},{16,24},{20,28},{24,16},{28,20},{32,40},... | collective-permute-start | bytes 1572872 | tf_op jit(solution)/shard_map/ppermute | solution.py:24
  263.8 12.1 %collective-permute-start.31 = (f32[4,128,4]{1,2,0:T(4,128)S(1)}, f32[4,128,4]{1,2,0:T(4,128)S(1)}, u32[]{:S(2)}, u32[]{:S(2)}) collective-permute-start(f32[4,128,4]{1,2,0:T(4,128)S(1)} %bitcast.237), channel_id=1, source_target_pairs={{0,8},{4,12},{8,0},{12,4},{16,24},{20,28},{24,16},{28,20},{32,40},... | collective-permute-start | bytes 24584 | tf_op jit(solution)/shard_map/ppermute | solution.py:24
  264.0 12.0 %collective-permute-start.21 = (f32[4,128,4]{1,2,0:T(4,128)S(1)}, f32[4,128,4]{1,2,0:T(4,128)S(1)}, u32[]{:S(2)}, u32[]{:S(2)}) collective-permute-start(f32[4,128,4]{1,2,0:T(4,128)S(1)} %bitcast.238), channel_id=1, source_target_pairs={{0,8},{4,12},{8,0},{12,4},{16,24},{20,28},{24,16},{28,20},{32,40},... | collective-permute-start | bytes 24584 | tf_op jit(solution)/shard_map/ppermute | solution.py:24
  276.2 14.4 %collective-permute-start.22 = (f32[4,128,4,64]{1,3,2,0:T(8,128)S(1)}, f32[4,128,4,64]{1,3,2,0:T(8,128)S(1)}, u32[]{:S(2)}, u32[]{:S(2)}) collective-permute-start(f32[4,128,4,64]{1,3,2,0:T(8,128)S(1)} %multiply_add_fusion.3), channel_id=1, source_target_pairs={{0,16},{4,20},{8,24},{12,28},{16,0},{20,4},{24,8},{28,12},{32,48},... | collective-permute-start | bytes 1572872 | tf_op jit(solution)/shard_map/ppermute | solution.py:24
  290.8 11.9 %collective-permute-start.24 = (f32[4,128,4,64]{1,3,2,0:T(8,128)S(1)}, f32[4,128,4,64]{1,3,2,0:T(8,128)S(1)}, u32[]{:S(2)}, u32[]{:S(2)}) collective-permute-start(f32[4,128,4,64]{1,3,2,0:T(8,128)S(1)} %multiply_add_fusion.2), channel_id=1, source_target_pairs={{0,32},{4,36},{8,40},{12,44},{16,48},{20,52},{24,56},{28,60},{32,0... | collective-permute-start | bytes 1572872 | tf_op jit(solution)/shard_map/ppermute | solution.py:24
  302.8 25.8 %collective-permute-start.26 = (f32[4,128,4,64]{1,3,2,0:T(8,128)S(1)}, f32[4,128,4,64]{1,3,2,0:T(8,128)S(1)}, u32[]{:S(2)}, u32[]{:S(2)}) collective-permute-start(f32[4,128,4,64]{1,3,2,0:T(8,128)S(1)} %multiply_add_fusion.1), channel_id=1, source_target_pairs={{0,64},{4,68},{8,72},{12,76},{16,80},{20,84},{24,88},{28,92},{32,9... | collective-permute-start | bytes 1572872 | tf_op jit(solution)/shard_map/ppermute | solution.py:24
  305.1 23.3 %collective-permute-start.34 = (f32[4,128,4]{1,2,0:T(4,128)S(1)}, f32[4,128,4]{1,2,0:T(4,128)S(1)}, u32[]{:S(2)}, u32[]{:S(2)}) collective-permute-start(f32[4,128,4]{1,2,0:T(4,128)S(1)} %bitcast.243), channel_id=1, source_target_pairs={{0,64},{4,68},{8,72},{12,76},{16,80},{20,84},{24,88},{28,92},{32,9... | collective-permute-start | bytes 24584 | tf_op jit(solution)/shard_map/ppermute | solution.py:24
  305.2 23.3 %collective-permute-start.27 = (f32[4,128,4]{1,2,0:T(4,128)S(1)}, f32[4,128,4]{1,2,0:T(4,128)S(1)}, u32[]{:S(2)}, u32[]{:S(2)}) collective-permute-start(f32[4,128,4]{1,2,0:T(4,128)S(1)} %bitcast.244), channel_id=1, source_target_pairs={{0,64},{4,68},{8,72},{12,76},{16,80},{20,84},{24,88},{28,92},{32,9... | collective-permute-start | bytes 24584 | tf_op jit(solution)/shard_map/ppermute | solution.py:24
  328.7 30.0 %collective-permute-start.28 = (f32[4,128,4,64]{1,3,2,0:T(8,128)S(1)}, f32[4,128,4,64]{1,3,2,0:T(8,128)S(1)}, u32[]{:S(2)}, u32[]{:S(2)}) collective-permute-start(f32[4,128,4,64]{1,3,2,0:T(8,128)S(1)} %multiply_add_fusion), channel_id=1, source_target_pairs={{0,128},{4,132},{8,136},{12,140},{16,144},{20,148},{24,152},{28,15... | collective-permute-start | bytes 1572872 | tf_op jit(solution)/shard_map/ppermute | solution.py:24
  335.2 23.4 %collective-permute-start.35 = (f32[4,128,4]{1,2,0:T(4,128)S(1)}, f32[4,128,4]{1,2,0:T(4,128)S(1)}, u32[]{:S(2)}, u32[]{:S(2)}) collective-permute-start(f32[4,128,4]{1,2,0:T(4,128)S(1)} %bitcast.223), channel_id=1, source_target_pairs={{0,128},{4,132},{8,136},{12,140},{16,144},{20,148},{24,152},{28,15... | collective-permute-start | bytes 24584 | tf_op jit(solution)/shard_map/ppermute | solution.py:24
  335.3 23.5 %collective-permute-start.29 = (f32[4,128,4]{1,2,0:T(4,128)S(1)}, f32[4,128,4]{1,2,0:T(4,128)S(1)}, u32[]{:S(2)}, u32[]{:S(2)}) collective-permute-start(f32[4,128,4]{1,2,0:T(4,128)S(1)} %bitcast.224), channel_id=1, source_target_pairs={{0,128},{4,132},{8,136},{12,140},{16,144},{20,148},{24,152},{28,15... | collective-permute-start | bytes 24584 | tf_op jit(solution)/shard_map/ppermute | solution.py:24
  361.1 138.3 %all-reduce.8.cloned.1.call-start = ((), (), s32[]{:S(2)}) async-start(), calls=%async_computation.3 | async-start | bytes 4194304 | tf_op jit(solution)/shard_map/psum | solution.py:44
  (33 other events, 883.8 us)
Sparse Core Ops, SparseCore 0:
  9.1 30.0 all-gather.1
  175.4 62.4 all-reduce.3
  361.2 61.2 all-reduce.5
  435.8 63.5 all-reduce.7
